TPU v7x, 32 devices: a whole 2x2x4 slice. The times are simulated.
32 devices in a mesh: dp: 8 (over z, y), seq: 4 (over x, core).
Axes of the slice: x: 2, y: 2, z: 4, core: 2. Of those that a mesh axis runs over, the one named last changes fastest.
Arguments:
- frames: bfloat16 [8, 512, 1536], P('dp', 'seq'), may hold values from -6 to 6
- lengths: int32 [8, 4], P('dp'), may hold values from 1 to 256, 512 in all within a row
- ln1_gain: float32 [1536], replicated, may hold values from 0.5 to 12
- ln2_gain: float32 [1536], replicated, may hold values from 0.5 to 1.5
- w_qkv: bfloat16 [1536, 3, 1536], P('dp', None, 'seq'), may hold values from -0.15625 to 0.15625
- w_out: bfloat16 [1536, 1536], P('seq', 'dp'), may hold values from -0.15625 to 0.15625
- w_glu: bfloat16 [1536, 2, 1536], P('dp', None, 'seq'), may hold values from -0.15625 to 0.15625
- dw_kernel: bfloat16 [31, 1536], P(None, 'seq'), may hold values from -1 to 1
- w_proj: bfloat16 [1536, 1536], P('seq', 'dp'), may hold values from -0.15625 to 0.15625
Outputs:
- block_out: bfloat16 [8, 512, 1536], P('dp', 'seq')
Inputs may be any that keep to these rules, and one draw needn't show every extreme that they name: `lengths`: each row sums to 512, and its largest entry is 256.
All inputs are finite; a program needn't handle non-finite values.
Results may differ from a plain program's by a relative error of at most 0.013.
The roundings to bfloat16 on the way count: a program that leaves them out, or rounds other values in their place, can miss the bound.
Values may be sent and summed in bfloat16 or wider, within the bound.
No kernel may reach another device: no remote copies, remote signals or barrier semaphores. Data moves between devices by JAX's collectives and lax.ppermute only.
A program may use at most 64 MiB of HBM per device.

v0:
```python
import jax
import jax.numpy as jnp
from jax import lax
from jax.sharding import PartitionSpec as P

HD = 96


def layer_norm(values, gain_vec):
    mean_value = jnp.mean(values, axis=-1, keepdims=True)
    centered = values - mean_value
    variance = jnp.mean(centered * centered, axis=-1, keepdims=True)
    return (centered * lax.rsqrt(variance + 1e-05) * gain_vec).astype(jnp.bfloat16)


def segment_of(record_ends, positions):
    return jnp.sum((positions[:, None] >= record_ends[None, :]).astype(jnp.int32), axis=1)


def seq_gather(block):
    count = lax.axis_size("seq")
    me = lax.axis_index("seq")
    parts = [block]
    for shift in range(1, count):
        parts.append(lax.ppermute(block, "seq", [(i, (i - shift) % count) for i in range(count)]))
    ring = jnp.concatenate(parts + parts, axis=0)
    rows = block.shape[0]
    return lax.dynamic_slice_in_dim(ring, (count - me) % count * rows, count * rows, axis=0)


def seq_scatter_sum(full):
    count = lax.axis_size("seq")
    me = lax.axis_index("seq")
    rows = full.shape[0] // count
    total = lax.dynamic_slice_in_dim(full, me * rows, rows, axis=0).astype(jnp.float32)
    for shift in range(1, count):
        piece = lax.dynamic_slice_in_dim(full, (me + shift) % count * rows, rows, axis=0)
        got = lax.ppermute(piece, "seq", [(i, (i + shift) % count) for i in range(count)])
        total = total + got.astype(jnp.float32)
    return total


def attend(projected, seg_all, head_size):
    group_rows = projected.shape[0]
    block_rows = 512
    heads_here = projected.shape[2] // head_size
    split = projected.reshape(group_rows, 3, heads_here, head_size)
    queries = split[:, 0]
    keys = split[:, 1]
    values = split[:, 2]
    blocks = group_rows // block_rows
    scale = 1.0 / head_size**0.5

    def one_block(block_data):
        query_block, seg_block = block_data
        scores = (
            jnp.einsum("qhe,khe->hqk", query_block, keys, preferred_element_type=jnp.float32)
            * scale
        )
        allowed = seg_block[:, None] == seg_all[None, :]
        scores = jnp.where(allowed[None], scores, -1e30)
        top_score = jnp.max(scores, axis=-1, keepdims=True)
        weights = jnp.exp(scores - top_score)
        probs = (weights / jnp.sum(weights, axis=-1, keepdims=True)).astype(jnp.bfloat16)
        mixed = jnp.einsum("hqk,khe->qhe", probs, values, preferred_element_type=jnp.float32)
        return mixed.astype(jnp.bfloat16).reshape(block_rows, heads_here * head_size)

    result = lax.map(
        one_block,
        (
            queries.reshape(blocks, block_rows, heads_here, head_size),
            seg_all.reshape(blocks, block_rows),
        ),
    )
    return result.reshape(group_rows, heads_here * head_size)


def depthwise(padded, kernel, seg_here, seg_near, count):
    total_acc = jnp.zeros((count, padded.shape[1]), jnp.float32)
    for tap_index in range(kernel.shape[0]):
        window = padded[tap_index : tap_index + count].astype(jnp.float32)
        same = (seg_near[tap_index : tap_index + count] == seg_here)[:, None]
        total_acc = total_acc + jnp.where(same, window * kernel[tap_index].astype(jnp.float32), 0.0)
    return jax.nn.silu(total_acc).astype(jnp.bfloat16)


def on_device(frames, lengths, ln1_gain, ln2_gain, w_qkv, w_out, w_glu, dw_kernel, w_proj):
    frame_rows = frames.shape[1]
    model_width = frames.shape[2]
    seq_count = lax.axis_size("seq")
    group_rows = frame_rows * seq_count
    group_width = model_width // seq_count
    kernel_reach = dw_kernel.shape[0] // 2
    qkv_matrix = lax.all_gather(
        w_qkv.reshape(w_qkv.shape[0], 3 * group_width), "dp", axis=0, tiled=True
    )
    out_local = lax.all_gather(w_out, "dp", axis=1, tiled=True)
    glu_matrix = lax.all_gather(
        w_glu.reshape(w_glu.shape[0], 2 * group_width), "dp", axis=0, tiled=True
    )
    proj_local = lax.all_gather(w_proj, "dp", axis=1, tiled=True)
    inputs = frames[0].astype(jnp.float32)
    record_ends = jnp.cumsum(lengths[0])
    seg_all = segment_of(record_ends, jnp.arange(group_rows, dtype=jnp.int32))
    normed1 = layer_norm(inputs, ln1_gain)
    projected = (
        jnp.dot(seq_gather(normed1), qkv_matrix, preferred_element_type=jnp.float32)
        .astype(jnp.bfloat16)
        .reshape(group_rows, 3, group_width)
    )
    attended = attend(projected, seg_all, HD)
    attn_sum = seq_scatter_sum(
        jnp.dot(attended, out_local, preferred_element_type=jnp.float32).astype(jnp.bfloat16)
    )
    middle = (inputs + attn_sum).astype(jnp.bfloat16)
    normed2 = layer_norm(middle.astype(jnp.float32), ln2_gain)
    shard_piece = seq_gather(normed2)
    paired = jnp.dot(shard_piece, glu_matrix, preferred_element_type=jnp.float32).reshape(
        shard_piece.shape[0], 2, group_width
    )
    gated = (paired[:, 0] * jax.nn.sigmoid(paired[:, 1])).astype(jnp.bfloat16)
    padded = jnp.pad(gated, ((kernel_reach, kernel_reach), (0, 0)))
    near_positions = jnp.arange(-kernel_reach, group_rows + kernel_reach, dtype=jnp.int32)
    activated = depthwise(
        padded, dw_kernel, seg_all, segment_of(record_ends, near_positions), group_rows
    )
    conv_out = seq_scatter_sum(
        jnp.dot(activated, proj_local, preferred_element_type=jnp.float32).astype(jnp.bfloat16)
    )
    results = [(middle.astype(jnp.float32) + conv_out).astype(jnp.bfloat16)]
    return jnp.stack(results, axis=0)


def solution(mesh):
    in_specs = (
        P("dp", "seq", None),
        P("dp", None),
        P(),
        P(),
        P("dp", None, "seq"),
        P("seq", "dp"),
        P("dp", None, "seq"),
        P(None, "seq"),
        P("seq", "dp"),
    )
    out_specs = P("dp", "seq", None)
    return jax.shard_map(
        on_device, mesh=mesh, in_specs=in_specs, out_specs=out_specs, check_vma=False
    )
```

profile of v0, /device:TPU:1, one launch (start us, length us, event | category | flops | bytes accessed | tf_op | source)
XLA Modules:
  0.0 247.0 jit_solution(16871168828461402253)
XLA Ops:
  6.5 1.9 copy.27
  8.5 0.7 all-gather.7.cloned.1.call-update
  9.2 1.7 copy.28
  11.0 1.1 convert_reduce_fusion.1
  12.2 1.2 fusion.19
  13.4 0.9 constant_dynamic-update-slice_fusion.7
  14.4 2.7 %collective-permute-start.1 = (bf16[128,1536]{1,0:T(8,128)(2,1)S(1)}, bf16[128,1536]{1,0:T(8,128)(2,1)S(1)}, u32[]{:S(2)}, u32[]{:S(2)}) collective-permute-start(bf16[128,1536]{1,0:T(8,128)(2,1)S(1)} %get-tuple-element.62), channel_id=1, source_target_pairs={{0,2},{1,3},{2,0},{3,1},{4,6},{5,7},{6,4},{7,5},{8,10},{9,11},{10,... | collective-permute-start | bytes 1179656 | tf_op jit(solution)/shard_map/ppermute | solution.py:25
  17.1 1.4 collective-permute-start.2
  18.5 0.2 reduce-window.8
  18.8 0.2 broadcast_compare_fusion
  19.0 8.0 %collective-permute-done = bf16[128,1536]{1,0:T(8,128)(2,1)S(1)} collective-permute-done((bf16[128,1536]{1,0:T(8,128)(2,1)S(1)}, bf16[128,1536]{1,0:T(8,128)(2,1)S(1)}, u32[]{:S(2)}, u32[]{:S(2)}) %collective-permute-start) | collective-permute-done | bytes 393248 | tf_op jit(solution)/shard_map/ppermute | solution.py:25
  27.0 0.8 constant_dynamic-update-slice_fusion.6
  27.8 0.8 constant_dynamic-update-slice_fusion.5
  28.6 5.9 %collective-permute-done.2 = bf16[128,1536]{1,0:T(8,128)(2,1)S(1)} collective-permute-done((bf16[128,1536]{1,0:T(8,128)(2,1)S(1)}, bf16[128,1536]{1,0:T(8,128)(2,1)S(1)}, u32[]{:S(2)}, u32[]{:S(2)}) %collective-permute-start.2) | collective-permute-done | bytes 393248 | tf_op jit(solution)/shard_map/ppermute | solution.py:25
  34.5 0.8 constant_dynamic-update-slice_fusion.4
  35.2 0.8 constant_dynamic-update-slice_fusion.3
  36.0 0.8 constant_dynamic-update-slice_fusion.2
  36.8 0.8 constant_dynamic-update-slice_fusion.1
  37.6 0.8 constant_dynamic-update-slice_fusion
  38.4 37.5 %all-gather.5.cloned.1.call-done = bf16[1536,1152]{1,0:T(8,128)(2,1)} async-done(((bf16[192,1152]{1,0:T(8,128)(2,1)}), bf16[1536,1152]{1,0:T(8,128)(2,1)}) %all-gather.5.cloned.1.call-update) | async-done | bytes 3538960 | tf_op jit(solution)/shard_map/all_gather | solution.py:94
  75.9 4.7 %convolution_convert_fusion = bf16[512,1152]{1,0:T(8,128)(2,1)S(1)} fusion(bf16[1536,1152]{1,0:T(8,128)(2,1)} %all-gather.5.cloned.1.call-done, bf16[1024,1536]{1,0:T(8,128)(2,1)} %constant_dynamic-update-slice_fusion, s32[]{:T(128)S(6)} %select_n.147), kind=kOutput, calls=%fused_computation.5 | convolution fusion | flops 1812529152 | bytes 6291460 | tf_op jit(solution)/shard_map/dot_general | solution.py:107
  80.6 0.6 copy.20
  81.2 3.6 %fusion.45 = (f32[4,512]{1,0:T(4,128)S(1)}, f32[4,512,512]{1,2,0:T(8,128)}) fusion(pred[512,512]{0,1:T(8,128)(4,1)S(1)} %broadcast_compare_fusion, bf16[512,3,4,96]{0,3,2,1:T(8,128)(2,1)S(1)} %bitcast.65), kind=kOutput, calls=%fused_computation.155 | convolution fusion | flops 205521408 | bytes 5251072 | tf_op jit(solution)/shard_map/while/body/eval_jaxpr/sub | solution.py:63
  84.8 2.8 %fusion.9 = bf16[4,96,512]{2,1,0:T(8,128)(2,1)S(1)} fusion(f32[4,512,512]{1,2,0:T(8,128)} %get-tuple-element.103, f32[4,512]{1,0:T(4,128)S(1)} %get-tuple-element.102, bf16[512,3,4,96]{0,3,2,1:T(8,128)(2,1)S(1)} %bitcast.66), kind=kOutput, calls=%fused_computation.15 | convolution fusion | flops 203620352 | bytes 4988928 | tf_op jit(solution)/shard_map/while/body/eval_jaxpr/hqk,khe->qhe/dot_general | solution.py:65
  87.6 29.8 %all-gather.7.cloned.1.call-done = bf16[384,1536]{0,1:T(8,128)(2,1)} async-done(((bf16[384,192]{0,1:T(8,128)(2,1)}), bf16[384,1536]{0,1:T(8,128)(2,1)}) %all-gather.7.cloned.1.call-update) | async-done | bytes 1179664 | tf_op jit(solution)/shard_map/all_gather | solution.py:97
  117.4 2.3 convolution_convert_fusion.2
  119.7 0.1 constant_dynamic-slice_fusion.5
  119.8 3.1 %collective-permute-start.3 = (bf16[128,1536]{1,0:T(8,128)(2,1)S(1)}, bf16[128,1536]{1,0:T(8,128)(2,1)S(1)}, u32[]{:S(2)}, u32[]{:S(2)}) collective-permute-start(bf16[128,1536]{1,0:T(8,128)(2,1)S(1)} %get-tuple-element.68), channel_id=1, source_target_pairs={{0,1},{1,2},{2,3},{3,0},{4,5},{5,6},{6,7},{7,4},{8,9},{9,10},{10,1... | collective-permute-start | bytes 1179656 | tf_op jit(solution)/shard_map/ppermute | solution.py:38
  122.8 0.3 collective-permute-start.4
  123.1 0.2 collective-permute-start.5
  123.3 0.7 convert_reduce_fusion.2
  124.0 0.7 slice_compare_fusion.30
  124.7 6.4 %collective-permute-done.3 = bf16[128,1536]{1,0:T(8,128)(2,1)S(1)} collective-permute-done((bf16[128,1536]{1,0:T(8,128)(2,1)S(1)}, bf16[128,1536]{1,0:T(8,128)(2,1)S(1)}, u32[]{:S(2)}, u32[]{:S(2)}) %collective-permute-start.3) | collective-permute-done | bytes 393248 | tf_op jit(solution)/shard_map/ppermute | solution.py:38
  131.2 9.5 %collective-permute-done.4 = bf16[128,1536]{1,0:T(8,128)(2,1)} collective-permute-done((bf16[128,1536]{1,0:T(8,128)(2,1)S(1)}, bf16[128,1536]{1,0:T(8,128)(2,1)}, u32[]{:S(2)}, u32[]{:S(2)}) %collective-permute-start.4) | collective-permute-done | bytes 393248 | tf_op jit(solution)/shard_map/ppermute | solution.py:38
  140.7 0.6 collective-permute-done.5
  141.3 1.5 convert_reduce_fusion
  142.8 0.3 fusion.16
  143.1 0.9 constant_dynamic-update-slice_fusion.15
  144.1 1.3 collective-permute-start.7
  145.4 0.1 convert_reduce_fusion.34
  145.5 2.2 collective-permute-start.8
  147.8 8.0 %collective-permute-done.6 = bf16[128,1536]{1,0:T(8,128)(2,1)S(1)} collective-permute-done((bf16[128,1536]{1,0:T(8,128)(2,1)S(1)}, bf16[128,1536]{1,0:T(8,128)(2,1)S(1)}, u32[]{:S(2)}, u32[]{:S(2)}) %collective-permute-start.6) | collective-permute-done | bytes 393248 | tf_op jit(solution)/shard_map/ppermute | solution.py:25
  155.7 0.8 constant_dynamic-update-slice_fusion.14
  156.5 0.8 constant_dynamic-update-slice_fusion.13
  157.3 5.1 %collective-permute-done.8 = bf16[128,1536]{1,0:T(8,128)(2,1)S(1)} collective-permute-done((bf16[128,1536]{1,0:T(8,128)(2,1)S(1)}, bf16[128,1536]{1,0:T(8,128)(2,1)S(1)}, u32[]{:S(2)}, u32[]{:S(2)}) %collective-permute-start.8) | collective-permute-done | bytes 393248 | tf_op jit(solution)/shard_map/ppermute | solution.py:25
  162.4 0.8 constant_dynamic-update-slice_fusion.12
  163.2 0.8 constant_dynamic-update-slice_fusion.11
  163.9 0.8 constant_dynamic-update-slice_fusion.10
  164.7 0.8 constant_dynamic-update-slice_fusion.9
  165.5 0.8 constant_dynamic-update-slice_fusion.8
  166.3 4.2 %all-gather.9.cloned.1.call-done = bf16[1536,768]{1,0:T(8,128)(2,1)} async-done(((bf16[192,768]{1,0:T(8,128)(2,1)}), bf16[1536,768]{1,0:T(8,128)(2,1)}) %all-gather.9.cloned.1.call-update) | async-done | bytes 2359312 | tf_op jit(solution)/shard_map/all_gather | solution.py:98
  170.5 4.7 %fusion.6 = f32[512,768]{1,0:T(8,128)} fusion(bf16[1536,768]{1,0:T(8,128)(2,1)} %all-gather.9.cloned.1.call-done, bf16[1024,1536]{1,0:T(8,128)(2,1)} %constant_dynamic-update-slice_fusion.8, s32[]{:T(128)S(6)} %select_n.147), kind=kOutput, calls=%fused_computation.12 | convolution fusion | flops 1207959552 | bytes 5505028 | tf_op jit(solution)/shard_map/dot_general | solution.py:118
  175.1 2.1 reshape.147
  177.5 1.2 fusion.44
  178.7 0.2 fusion.32
  178.9 33.2 %all-gather.11.cloned.1.call-done = bf16[384,1536]{0,1:T(8,128)(2,1)} async-done(((bf16[384,192]{0,1:T(8,128)(2,1)}), bf16[384,1536]{0,1:T(8,128)(2,1)}) %all-gather.11.cloned.1.call-update) | async-done | bytes 1179664 | tf_op jit(solution)/shard_map/all_gather | solution.py:101
  212.2 7.8 %convolution_convert_fusion.1 = bf16[512,1536]{1,0:T(8,128)(2,1)S(1)} fusion(bf16[384,1536]{0,1:T(8,128)(2,1)} %all-gather.11.cloned.1.call-done, bf16[512,384]{1,0:T(8,128)(2,1)S(1)} %fusion.32, f32[384]{0:T(512)S(1)} %get-tuple-element.55, f32[384]{0:T(512)S(1)} %get-tuple-element.56, f32[384]{0:T(512)S(1)} %get-tuple-element.18, ...), kind=kOutput, calls=%fused_computation.6 | convolution fusion | flops 629932032 | bytes 3209216 | tf_op jit(solution)/shard_map/dot_general | solution.py:128
  220.1 0.1 constant_dynamic-slice_fusion.2
  220.2 1.3 collective-permute-start.10
  221.4 2.2 collective-permute-start.11
  223.6 0.2 collective-permute-start.9
  223.8 5.1 %collective-permute-done.10 = bf16[128,1536]{1,0:T(8,128)(2,1)S(1)} collective-permute-done((bf16[128,1536]{1,0:T(8,128)(2,1)S(1)}, bf16[128,1536]{1,0:T(8,128)(2,1)S(1)}, u32[]{:S(2)}, u32[]{:S(2)}) %collective-permute-start.10) | collective-permute-done | bytes 393248 | tf_op jit(solution)/shard_map/ppermute | solution.py:38
  228.9 10.6 %collective-permute-done.11 = bf16[128,1536]{1,0:T(8,128)(2,1)S(1)} collective-permute-done((bf16[128,1536]{1,0:T(8,128)(2,1)S(1)}, bf16[128,1536]{1,0:T(8,128)(2,1)S(1)}, u32[]{:S(2)}, u32[]{:S(2)}) %collective-permute-start.11) | collective-permute-done | bytes 393248 | tf_op jit(solution)/shard_map/ppermute | solution.py:38
  239.5 1.0 fusion.31
  (68 shorter events, 0.6 us)
Async XLA Ops:
  6.5 6.9 %copy-start = (bf16[1,128,1536]{2,1,0:T(8,128)(2,1)S(1)}, bf16[1,128,1536]{2,1,0:T(8,128)(2,1)}, u32[]{:S(2)}) copy-start(bf16[1,128,1536]{2,1,0:T(8,128)(2,1)} %param.9) | copy-start | bytes 1179652
  6.5 6.9 %copy-start.2 = (f32[1536]{0:T(1024)S(1)}, f32[1536]{0:T(1024)}, u32[]{:S(2)}) copy-start(f32[1536]{0:T(1024)} %param.11) | copy-start | bytes 18436
  6.5 12.0 %copy-start.23 = (s32[1,4]{1,0:T(1,128)S(1)}, s32[1,4]{1,0:T(1,128)}, u32[]{:S(2)}) copy-start(s32[1,4]{1,0:T(1,128)} %param.10) | copy-start | bytes 52
  6.5 69.3 %all-gather.5.cloned.1.call-start = ((), (), s32[]{:S(2)}) async-start(), calls=%async_computation | async-start | bytes 3981312 | tf_op jit(solution)/shard_map/all_gather | solution.py:94
  8.4 108.9 %all-gather.7.cloned.1.call-start = ((), (), s32[]{:S(2)}) async-start(), calls=%async_computation.1 | async-start | bytes 1327104 | tf_op jit(solution)/shard_map/all_gather | solution.py:97
  9.2 161.3 %all-gather.9.cloned.1.call-start = ((), (), s32[]{:S(2)}) async-start(), calls=%async_computation.2 | async-start | bytes 2654208 | tf_op jit(solution)/shard_map/all_gather | solution.py:98
  11.0 201.1 %all-gather.11.cloned.1.call-start = ((), (), s32[]{:S(2)}) async-start(), calls=%async_computation.3 | async-start | bytes 1327104 | tf_op jit(solution)/shard_map/all_gather | solution.py:101
  14.4 12.7 %collective-permute-start = (bf16[128,1536]{1,0:T(8,128)(2,1)S(1)}, bf16[128,1536]{1,0:T(8,128)(2,1)S(1)}, u32[]{:S(2)}, u32[]{:S(2)}) collective-permute-start(bf16[128,1536]{1,0:T(8,128)(2,1)S(1)} %get-tuple-element.62), channel_id=1, source_target_pairs={{0,3},{1,0},{2,1},{3,2},{4,7},{5,4},{6,5},{7,6},{8,11},{9,8},{10,9... | collective-permute-start | bytes 1179656 | tf_op jit(solution)/shard_map/ppermute | solution.py:25
  14.4 13.4 %collective-permute-start.1 = (bf16[128,1536]{1,0:T(8,128)(2,1)S(1)}, bf16[128,1536]{1,0:T(8,128)(2,1)S(1)}, u32[]{:S(2)}, u32[]{:S(2)}) collective-permute-start(bf16[128,1536]{1,0:T(8,128)(2,1)S(1)} %get-tuple-element.62), channel_id=1, source_target_pairs={{0,2},{1,3},{2,0},{3,1},{4,6},{5,7},{6,4},{7,5},{8,10},{9,11},{10,... | collective-permute-start | bytes 1179656 | tf_op jit(solution)/shard_map/ppermute | solution.py:25
  17.1 17.4 %collective-permute-start.2 = (bf16[128,1536]{1,0:T(8,128)(2,1)S(1)}, bf16[128,1536]{1,0:T(8,128)(2,1)S(1)}, u32[]{:S(2)}, u32[]{:S(2)}) collective-permute-start(bf16[128,1536]{1,0:T(8,128)(2,1)S(1)} %get-tuple-element.62), channel_id=1, source_target_pairs={{0,1},{1,2},{2,3},{3,0},{4,5},{5,6},{6,7},{7,4},{8,9},{9,10},{10,1... | collective-permute-start | bytes 1179656 | tf_op jit(solution)/shard_map/ppermute | solution.py:25
  18.7 19.7 %copy-start.4 = (s32[4,1]{0,1:T(1,128)}, s32[4,1]{0,1:T(1,128)S(1)}, u32[]{:S(2)}) copy-start(s32[4,1]{0,1:T(1,128)S(1)} %reduce-window.8) | copy-start | bytes 52
  119.7 23.4 %copy-start.3 = (f32[1536]{0:T(1024)S(1)}, f32[1536]{0:T(1024)}, u32[]{:S(2)}) copy-start(f32[1536]{0:T(1024)} %param.12) | copy-start | bytes 18436
  119.8 11.4 %collective-permute-start.3 = (bf16[128,1536]{1,0:T(8,128)(2,1)S(1)}, bf16[128,1536]{1,0:T(8,128)(2,1)S(1)}, u32[]{:S(2)}, u32[]{:S(2)}) collective-permute-start(bf16[128,1536]{1,0:T(8,128)(2,1)S(1)} %get-tuple-element.68), channel_id=1, source_target_pairs={{0,1},{1,2},{2,3},{3,0},{4,5},{5,6},{6,7},{7,4},{8,9},{9,10},{10,1... | collective-permute-start | bytes 1179656 | tf_op jit(solution)/shard_map/ppermute | solution.py:38
  122.8 17.9 %collective-permute-start.4 = (bf16[128,1536]{1,0:T(8,128)(2,1)S(1)}, bf16[128,1536]{1,0:T(8,128)(2,1)}, u32[]{:S(2)}, u32[]{:S(2)}) collective-permute-start(bf16[128,1536]{1,0:T(8,128)(2,1)S(1)} %get-tuple-element.70), channel_id=1, source_target_pairs={{0,2},{1,3},{2,0},{3,1},{4,6},{5,7},{6,4},{7,5},{8,10},{9,11},{10,... | collective-permute-start | bytes 1179656 | tf_op jit(solution)/shard_map/ppermute | solution.py:38
  123.1 18.2 %collective-permute-start.5 = (bf16[128,1536]{1,0:T(8,128)(2,1)S(1)}, bf16[128,1536]{1,0:T(8,128)(2,1)}, u32[]{:S(2)}, u32[]{:S(2)}) collective-permute-start(bf16[128,1536]{1,0:T(8,128)(2,1)S(1)} %get-tuple-element.69), channel_id=1, source_target_pairs={{0,3},{1,0},{2,1},{3,2},{4,7},{5,4},{6,5},{7,6},{8,11},{9,8},{10,9... | collective-permute-start | bytes 1179656 | tf_op jit(solution)/shard_map/ppermute | solution.py:38
  123.3 22.0 %copy-start.1 = (bf16[31,384]{1,0:T(8,128)(2,1)S(1)}, bf16[31,384]{1,0:T(8,128)(2,1)}, u32[]{:S(2)}) copy-start(bf16[31,384]{1,0:T(8,128)(2,1)} %param.16) | copy-start | bytes 71428
  144.0 11.7 %collective-permute-start.6 = (bf16[128,1536]{1,0:T(8,128)(2,1)S(1)}, bf16[128,1536]{1,0:T(8,128)(2,1)S(1)}, u32[]{:S(2)}, u32[]{:S(2)}) collective-permute-start(bf16[128,1536]{1,0:T(8,128)(2,1)S(1)} %get-tuple-element.58), channel_id=1, source_target_pairs={{0,3},{1,0},{2,1},{3,2},{4,7},{5,4},{6,5},{7,6},{8,11},{9,8},{10,9... | collective-permute-start | bytes 1179656 | tf_op jit(solution)/shard_map/ppermute | solution.py:25
  144.1 12.4 %collective-permute-start.7 = (bf16[128,1536]{1,0:T(8,128)(2,1)S(1)}, bf16[128,1536]{1,0:T(8,128)(2,1)S(1)}, u32[]{:S(2)}, u32[]{:S(2)}) collective-permute-start(bf16[128,1536]{1,0:T(8,128)(2,1)S(1)} %get-tuple-element.58), channel_id=1, source_target_pairs={{0,2},{1,3},{2,0},{3,1},{4,6},{5,7},{6,4},{7,5},{8,10},{9,11},{10,... | collective-permute-start | bytes 1179656 | tf_op jit(solution)/shard_map/ppermute | solution.py:25
  145.5 16.9 %collective-permute-start.8 = (bf16[128,1536]{1,0:T(8,128)(2,1)S(1)}, bf16[128,1536]{1,0:T(8,128)(2,1)S(1)}, u32[]{:S(2)}, u32[]{:S(2)}) collective-permute-start(bf16[128,1536]{1,0:T(8,128)(2,1)S(1)} %get-tuple-element.58), channel_id=1, source_target_pairs={{0,1},{1,2},{2,3},{3,0},{4,5},{5,6},{6,7},{7,4},{8,9},{9,10},{10,1... | collective-permute-start | bytes 1179656 | tf_op jit(solution)/shard_map/ppermute | solution.py:25
  177.3 34.8 %copy-start.5 = (pred[512]{0:T(512)(128)(4,1)S(1)}, pred[512]{0:T(512)(128)(4,1)}, u32[]{:S(2)}) copy-start(pred[512]{0:T(512)(128)(4,1)} %get-tuple-element.71) | copy-start | bytes 1540
  177.3 34.8 %copy-start.6 = (pred[512]{0:T(512)(128)(4,1)S(1)}, pred[512]{0:T(512)(128)(4,1)}, u32[]{:S(2)}) copy-start(pred[512]{0:T(512)(128)(4,1)} %get-tuple-element.72) | copy-start | bytes 1540
  177.3 34.8 %copy-start.7 = (pred[512]{0:T(512)(128)(4,1)S(1)}, pred[512]{0:T(512)(128)(4,1)}, u32[]{:S(2)}) copy-start(pred[512]{0:T(512)(128)(4,1)} %get-tuple-element.73) | copy-start | bytes 1540
  177.3 34.8 %copy-start.8 = (pred[512]{0:T(512)(128)(4,1)S(1)}, pred[512]{0:T(512)(128)(4,1)}, u32[]{:S(2)}) copy-start(pred[512]{0:T(512)(128)(4,1)} %get-tuple-element.74) | copy-start | bytes 1540
  177.3 34.8 %copy-start.9 = (pred[512]{0:T(512)(128)(4,1)S(1)}, pred[512]{0:T(512)(128)(4,1)}, u32[]{:S(2)}) copy-start(pred[512]{0:T(512)(128)(4,1)} %get-tuple-element.75) | copy-start | bytes 1540
  177.3 34.8 %copy-start.10 = (pred[512]{0:T(512)(128)(4,1)S(1)}, pred[512]{0:T(512)(128)(4,1)}, u32[]{:S(2)}) copy-start(pred[512]{0:T(512)(128)(4,1)} %get-tuple-element.76) | copy-start | bytes 1540
  177.3 34.8 %copy-start.11 = (pred[512]{0:T(512)(128)(4,1)S(1)}, pred[512]{0:T(512)(128)(4,1)}, u32[]{:S(2)}) copy-start(pred[512]{0:T(512)(128)(4,1)} %get-tuple-element.77) | copy-start | bytes 1540
  177.3 34.8 %copy-start.12 = (pred[512]{0:T(512)(128)(4,1)S(1)}, pred[512]{0:T(512)(128)(4,1)}, u32[]{:S(2)}) copy-start(pred[512]{0:T(512)(128)(4,1)} %get-tuple-element.78) | copy-start | bytes 1540
  177.4 34.8 %copy-start.13 = (pred[512]{0:T(512)(128)(4,1)S(1)}, pred[512]{0:T(512)(128)(4,1)}, u32[]{:S(2)}) copy-start(pred[512]{0:T(512)(128)(4,1)} %get-tuple-element.79) | copy-start | bytes 1540
  177.4 34.8 %copy-start.14 = (pred[512]{0:T(512)(128)(4,1)S(1)}, pred[512]{0:T(512)(128)(4,1)}, u32[]{:S(2)}) copy-start(pred[512]{0:T(512)(128)(4,1)} %get-tuple-element.80) | copy-start | bytes 1540
  177.4 34.8 %copy-start.15 = (pred[512]{0:T(512)(128)(4,1)S(1)}, pred[512]{0:T(512)(128)(4,1)}, u32[]{:S(2)}) copy-start(pred[512]{0:T(512)(128)(4,1)} %get-tuple-element.81) | copy-start | bytes 1540
  177.4 34.8 %copy-start.16 = (pred[512]{0:T(512)(128)(4,1)S(1)}, pred[512]{0:T(512)(128)(4,1)}, u32[]{:S(2)}) copy-start(pred[512]{0:T(512)(128)(4,1)} %get-tuple-element.82) | copy-start | bytes 1540
  177.4 34.8 %copy-start.17 = (pred[512]{0:T(512)(128)(4,1)S(1)}, pred[512]{0:T(512)(128)(4,1)}, u32[]{:S(2)}) copy-start(pred[512]{0:T(512)(128)(4,1)} %get-tuple-element.83) | copy-start | bytes 1540
  177.4 34.8 %copy-start.18 = (pred[512]{0:T(512)(128)(4,1)S(1)}, pred[512]{0:T(512)(128)(4,1)}, u32[]{:S(2)}) copy-start(pred[512]{0:T(512)(128)(4,1)} %get-tuple-element.84) | copy-start | bytes 1540
  177.4 34.8 %copy-start.19 = (pred[512]{0:T(512)(128)(4,1)S(1)}, pred[512]{0:T(512)(128)(4,1)}, u32[]{:S(2)}) copy-start(pred[512]{0:T(512)(128)(4,1)} %get-tuple-element.85) | copy-start | bytes 1540
  177.4 34.8 %copy-start.20 = (pred[512]{0:T(512)(128)(4,1)S(1)}, pred[512]{0:T(512)(128)(4,1)}, u32[]{:S(2)}) copy-start(pred[512]{0:T(512)(128)(4,1)} %get-tuple-element.86) | copy-start | bytes 1540
  177.4 34.8 %copy-start.21 = (pred[512]{0:T(512)(128)(4,1)S(1)}, pred[512]{0:T(512)(128)(4,1)}, u32[]{:S(2)}) copy-start(pred[512]{0:T(512)(128)(4,1)} %get-tuple-element.87) | copy-start | bytes 1540
  177.4 34.8 %copy-start.22 = (pred[512]{0:T(512)(128)(4,1)S(1)}, pred[512]{0:T(512)(128)(4,1)}, u32[]{:S(2)}) copy-start(pred[512]{0:T(512)(128)(4,1)} %get-tuple-element.88) | copy-start | bytes 1540
  220.2 8.7 %collective-permute-start.10 = (bf16[128,1536]{1,0:T(8,128)(2,1)S(1)}, bf16[128,1536]{1,0:T(8,128)(2,1)S(1)}, u32[]{:S(2)}, u32[]{:S(2)}) collective-permute-start(bf16[128,1536]{1,0:T(8,128)(2,1)S(1)} %get-tuple-element.65), channel_id=1, source_target_pairs={{0,2},{1,3},{2,0},{3,1},{4,6},{5,7},{6,4},{7,5},{8,10},{9,11},{10,... | collective-permute-start | bytes 1179656 | tf_op jit(solution)/shard_map/ppermute | solution.py:38
  221.4 18.1 %collective-permute-start.11 = (bf16[128,1536]{1,0:T(8,128)(2,1)S(1)}, bf16[128,1536]{1,0:T(8,128)(2,1)S(1)}, u32[]{:S(2)}, u32[]{:S(2)}) collective-permute-start(bf16[128,1536]{1,0:T(8,128)(2,1)S(1)} %get-tuple-element.64), channel_id=1, source_target_pairs={{0,3},{1,0},{2,1},{3,2},{4,7},{5,4},{6,5},{7,6},{8,11},{9,8},{10,9... | collective-permute-start | bytes 1179656 | tf_op jit(solution)/shard_map/ppermute | solution.py:38
  223.6 15.9 %collective-permute-start.9 = (bf16[128,1536]{1,0:T(8,128)(2,1)S(1)}, bf16[128,1536]{1,0:T(8,128)(2,1)S(1)}, u32[]{:S(2)}, u32[]{:S(2)}) collective-permute-start(bf16[128,1536]{1,0:T(8,128)(2,1)S(1)} %get-tuple-element.63), channel_id=1, source_target_pairs={{0,1},{1,2},{2,3},{3,0},{4,5},{5,6},{6,7},{7,4},{8,9},{9,10},{10,1... | collective-permute-start | bytes 1179656 | tf_op jit(solution)/shard_map/ppermute | solution.py:38
Sparse Core Ops, SparseCore 0:
  9.5 66.2 all-gather.4
  78.1 39.2 all-gather.6
  119.5 50.8 all-gather.8
  172.5 39.5 all-gather.10
where the time goes:
time: 247 us
  waiting for transfers between devices  165 us (67%)
  matrix products  25.8 us (10%)
  local copies, waits for them, and re-layouts  18.8 us (8%)
  starting transfers between devices  14.8 us (6%)
  between operations  13.6 us (6%)
  other arithmetic  9.38 us (4%)
    all_gather x1, waiting for transfers between devices, on_device(): lax.all_gather(w_qkv.reshape(w_qkv.shape[0], 3 * group_width), 'dp', axis...  37.5 us
    all_gather x1, waiting for transfers between devices, on_device(): proj_local = lax.all_gather(w_proj, 'dp', axis=1, tiled=True)  33.2 us
    ppermute x6, waiting for transfers between devices, seq_scatter_sum(): lax.ppermute(piece, 'seq', [(i, (i + shift) % count) for i in range(count)])  32.3 us
    all_gather x1, waiting for transfers between devices, on_device(): out_local = lax.all_gather(w_out, 'dp', axis=1, tiled=True)  29.8 us
    ppermute x6, waiting for transfers between devices, seq_gather(): lax.ppermute(block, 'seq', [(i, (i - shift) % count) for i in range(count)])  26.9 us
    unnamed x61, local copies, waits for them, and re-layouts  11.2 us
    dot_general x1, matrix products, on_device(): jnp.dot(activated, proj_local, preferred_element_type=jnp.float32)  7.81 us
    ppermute x6, starting transfers between devices, seq_gather(): lax.ppermute(block, 'seq', [(i, (i - shift) % count) for i in range(count)])  7.57 us
  transfers between devices with their start and end apart: 16, of which 13 were waited for; matrix products, arithmetic and copies ran while one was open for 17% of the time, Pallas kernels for 0%

commit v1 on v0

--- a/solution.py
+++ b/solution.py
@@ -1,9 +1,28 @@
+import functools
 import jax
 import jax.numpy as jnp
 from jax import lax
 from jax.sharding import PartitionSpec as P
 
 HD = 96
+
+
+def slot_bind(local_array, axis_name):
+    chips = lax.axis_size(axis_name)
+    queue = tuple(((dev_i, (dev_i + 1) % chips) for dev_i in range(chips)))
+    crops = tuple(((dev_i, (dev_i - 1) % chips) for dev_i in range(chips)))
+    main, tmp = ([local_array], [local_array])
+    for _ in range(chips // 2):
+        long_array = lax.ppermute(main[-1], axis_name, queue)
+        main.append(long_array)
+    for _ in range((chips - 1) // 2):
+        tmp.append(lax.ppermute(tmp[-1], axis_name, crops))
+    known = jnp.concatenate([*main[::-1], *tmp[1:]], axis=0)
+    left_arr = lax.axis_index(axis_name)
+    return jnp.roll(known, (left_arr - chips // 2) * local_array.shape[0], axis=0)
+
+
+enter_ticks_up = functools.partial(slot_bind, axis_name="dp")
 
 
 def layer_norm(values, gain_vec):
@@ -91,9 +110,7 @@
     group_rows = frame_rows * seq_count
     group_width = model_width // seq_count
     kernel_reach = dw_kernel.shape[0] // 2
-    qkv_matrix = lax.all_gather(
-        w_qkv.reshape(w_qkv.shape[0], 3 * group_width), "dp", axis=0, tiled=True
-    )
+    qkv_matrix = enter_ticks_up(w_qkv.reshape(w_qkv.shape[0], 3 * group_width))
     out_local = lax.all_gather(w_out, "dp", axis=1, tiled=True)
     glu_matrix = lax.all_gather(
         w_glu.reshape(w_glu.shape[0], 2 * group_width), "dp", axis=0, tiled=True

time: 247 us -> 213 us (0.86)
  waiting for transfers between devices: 165 us -> 116 us
  starting transfers between devices: 14.8 us -> 30.1 us
  matrix products: 25.8 us -> 22.5 us
  other arithmetic: 9.38 us -> 12.2 us
    ppermute x0 -> x7, waiting for transfers between devices: none -> 60.5 us  [the longest x4 56 us: slot_bind(): long_array = lax.ppermute(main[-1], axis_name, queue)]
    all_gather x1 -> x0, waiting for transfers between devices: 37.5 us -> none  [on_device(): lax.all_gather(w_qkv.reshape(w_qkv.shape[0], 3 * group_width), 'dp', axis...]
    all_gather x1, waiting for transfers between devices: 29.8 us -> 0.02 us  [on_device(): out_local = lax.all_gather(w_out, 'dp', axis=1, tiled=True)]
    all_gather x1, waiting for transfers between devices: 33.2 us -> 8.41 us  [on_device(): proj_local = lax.all_gather(w_proj, 'dp', axis=1, tiled=True)]
    ppermute x0 -> x7, starting transfers between devices: none -> 16.4 us  [the longest x3 9.18 us: slot_bind(): tmp.append(lax.ppermute(tmp[-1], axis_name, crops))]
    ppermute x6, waiting for transfers between devices: 26.9 us -> 12.3 us  [seq_gather(): lax.ppermute(block, 'seq', [(i, (i - shift) % count) for i in range(count)])]
    all_gather x1, waiting for transfers between devices: 4.18 us -> 0.01 us  [on_device(): lax.all_gather(w_glu.reshape(w_glu.shape[0], 2 * group_width), 'dp', axis...]
    unnamed x61 -> x122, local copies, waits for them, and re-layouts: 11.2 us -> 14 us
  transfers between devices with their start and end apart: 16 -> 22, of which waited for: 13 -> 15; matrix products, arithmetic and copies ran while one was open for 17% -> 20% of each run, Pallas kernels for 0% -> 0%
where the time goes in v1:
time: 213 us
  waiting for transfers between devices  116 us (54%)
  starting transfers between devices  30.1 us (14%)
  matrix products  22.5 us (11%)
  local copies, waits for them, and re-layouts  18.5 us (9%)
  between operations  14.1 us (7%)
  other arithmetic  12.2 us (6%)
    ppermute x4, waiting for transfers between devices, slot_bind(): long_array = lax.ppermute(main[-1], axis_name, queue)  56 us
    ppermute x6, waiting for transfers between devices, seq_scatter_sum(): lax.ppermute(piece, 'seq', [(i, (i + shift) % count) for i in range(count)])  33.6 us
    unnamed x122, local copies, waits for them, and re-layouts  14 us
    ppermute x6, waiting for transfers between devices, seq_gather(): lax.ppermute(block, 'seq', [(i, (i - shift) % count) for i in range(count)])  12.3 us
    ppermute x3, starting transfers between devices, slot_bind(): tmp.append(lax.ppermute(tmp[-1], axis_name, crops))  9.18 us
    all_gather x1, waiting for transfers between devices, on_device(): proj_local = lax.all_gather(w_proj, 'dp', axis=1, tiled=True)  8.41 us
    dot_general x1, matrix products, on_device(): jnp.dot(activated, proj_local, preferred_element_type=jnp.float32)  8.09 us
    ppermute x4, starting transfers between devices, slot_bind(): long_array = lax.ppermute(main[-1], axis_name, queue)  7.25 us
  transfers between devices with their start and end apart: 22, of which 15 were waited for; matrix products, arithmetic and copies ran while one was open for 20% of the time, Pallas kernels for 0%

profile of v1, /device:TPU:1, one launch (start us, length us, event | category | flops | bytes accessed | tf_op | source)
XLA Modules:
  0.0 213.0 jit_solution(2664017020576525598)
XLA Ops:
  6.5 0.7 all-gather.4.cloned.1.call-update
  7.3 1.7 copy.28
  9.1 1.1 convert_reduce_fusion.1
  10.2 1.2 fusion.24
  11.5 2.0 constant_dynamic-update-slice_fusion.7
  13.6 2.7 %collective-permute-start.3 = (bf16[192,1152]{1,0:T(8,128)(2,1)S(1)}, bf16[192,1152]{1,0:T(8,128)(2,1)S(1)}, u32[]{:S(2)}, u32[]{:S(2)}) collective-permute-start(bf16[192,1152]{1,0:T(8,128)(2,1)S(1)} %bitcast.63), channel_id=1, source_target_pairs={{0,4},{4,8},{8,12},{12,16},{16,20},{20,24},{24,28},{28,0},{1,5},{5... | collective-permute-start | bytes 1327112 | tf_op jit(solution)/shard_map/ppermute | solution.py:16
  16.3 3.1 %collective-permute-start.7 = (bf16[192,1152]{1,0:T(8,128)(2,1)S(1)}, bf16[192,1152]{1,0:T(8,128)(2,1)S(1)}, u32[]{:S(2)}, u32[]{:S(2)}) collective-permute-start(bf16[192,1152]{1,0:T(8,128)(2,1)S(1)} %bitcast.64), channel_id=1, source_target_pairs={{0,28},{4,0},{8,4},{12,8},{16,12},{20,16},{24,20},{28,24},{1,29},{... | collective-permute-start | bytes 1327112 | tf_op jit(solution)/shard_map/ppermute | solution.py:19
  19.4 1.2 collective-permute-start.1
  20.6 1.7 collective-permute-start.2
  22.6 0.5 copy-done.20
  23.5 0.8 constant_dynamic-update-slice_fusion.6
  24.3 11.6 %collective-permute-done.3 = bf16[192,1152]{1,0:T(8,128)(2,1)S(1)} collective-permute-done((bf16[192,1152]{1,0:T(8,128)(2,1)S(1)}, bf16[192,1152]{1,0:T(8,128)(2,1)S(1)}, u32[]{:S(2)}, u32[]{:S(2)}) %collective-permute-start.3) | collective-permute-done | bytes 442400 | tf_op jit(solution)/shard_map/ppermute | solution.py:16
  35.9 2.2 %collective-permute-start.4 = (bf16[192,1152]{1,0:T(8,128)(2,1)S(1)}, bf16[192,1152]{1,0:T(8,128)(2,1)S(1)}, u32[]{:S(2)}, u32[]{:S(2)}) collective-permute-start(bf16[192,1152]{1,0:T(8,128)(2,1)S(1)} %collective-permute-done.3), channel_id=1, source_target_pairs={{0,4},{4,8},{8,12},{12,16},{16,20},{20,24},{24,28},{28,0},{1,5},{5... | collective-permute-start | bytes 1327112 | tf_op jit(solution)/shard_map/ppermute | solution.py:16
  38.1 0.8 constant_dynamic-update-slice_fusion.5
  38.9 0.8 constant_dynamic-update-slice_fusion.4
  39.7 10.2 %collective-permute-done.4 = bf16[192,1152]{1,0:T(8,128)(2,1)S(1)} collective-permute-done((bf16[192,1152]{1,0:T(8,128)(2,1)S(1)}, bf16[192,1152]{1,0:T(8,128)(2,1)S(1)}, u32[]{:S(2)}, u32[]{:S(2)}) %collective-permute-start.4) | collective-permute-done | bytes 442400 | tf_op jit(solution)/shard_map/ppermute | solution.py:16
  49.9 0.8 constant_dynamic-update-slice_fusion.3
  50.7 0.8 constant_dynamic-update-slice_fusion.2
  51.5 4.2 %collective-permute-start.8 = (bf16[192,1152]{1,0:T(8,128)(2,1)S(1)}, bf16[192,1152]{1,0:T(8,128)(2,1)S(1)}, u32[]{:S(2)}, u32[]{:S(2)}) collective-permute-start(bf16[192,1152]{1,0:T(8,128)(2,1)S(1)} %collective-permute-done.7), channel_id=1, source_target_pairs={{0,28},{4,0},{8,4},{12,8},{16,12},{20,16},{24,20},{28,24},{1,29},{... | collective-permute-start | bytes 1327112 | tf_op jit(solution)/shard_map/ppermute | solution.py:19
  55.7 16.9 %collective-permute-done.5 = bf16[192,1152]{1,0:T(8,128)(2,1)S(1)} collective-permute-done((bf16[192,1152]{1,0:T(8,128)(2,1)S(1)}, bf16[192,1152]{1,0:T(8,128)(2,1)S(1)}, u32[]{:S(2)}, u32[]{:S(2)}) %collective-permute-start.5) | collective-permute-done | bytes 442400 | tf_op jit(solution)/shard_map/ppermute | solution.py:16
  72.5 2.3 %collective-permute-start.6 = (bf16[192,1152]{1,0:T(8,128)(2,1)S(1)}, bf16[192,1152]{1,0:T(8,128)(2,1)S(1)}, u32[]{:S(2)}, u32[]{:S(2)}) collective-permute-start(bf16[192,1152]{1,0:T(8,128)(2,1)S(1)} %collective-permute-done.5), channel_id=1, source_target_pairs={{0,4},{4,8},{8,12},{12,16},{16,20},{20,24},{24,28},{28,0},{1,5},{5... | collective-permute-start | bytes 1327112 | tf_op jit(solution)/shard_map/ppermute | solution.py:16
  74.8 0.8 constant_dynamic-update-slice_fusion.1
  75.6 0.8 constant_dynamic-update-slice_fusion
  76.6 1.9 collective-permute-start.9
  78.6 17.2 %collective-permute-done.6 = bf16[192,1152]{1,0:T(8,128)(2,1)S(1)} collective-permute-done((bf16[192,1152]{1,0:T(8,128)(2,1)S(1)}, bf16[192,1152]{1,0:T(8,128)(2,1)S(1)}, u32[]{:S(2)}, u32[]{:S(2)}) %collective-permute-start.6) | collective-permute-done | bytes 442400 | tf_op jit(solution)/shard_map/ppermute | solution.py:16
  96.1 4.2 %collective-permute-done.9 = bf16[192,1152]{1,0:T(8,128)(2,1)S(1)} collective-permute-done((bf16[192,1152]{1,0:T(8,128)(2,1)S(1)}, bf16[192,1152]{1,0:T(8,128)(2,1)S(1)}, u32[]{:S(2)}, u32[]{:S(2)}) %collective-permute-start.9) | collective-permute-done | bytes 442400 | tf_op jit(solution)/shard_map/ppermute | solution.py:19
  100.9 1.5 copy-done.3
  102.4 2.2 %fusion.4 = bf16[512,1152]{1,0:T(8,128)(2,1)S(1)} fusion(bf16[3072,1152]{1,0:T(8,128)(2,1)S(1)} %constant_dynamic-update-slice_fusion.8, s32[]{:T(128)S(6)} %select_n.161, bf16[1024,1536]{1,0:T(8,128)(2,1)S(1)} %copy-done.3, s32[]{:T(128)S(6)} %select_n.159), kind=kOutput, calls=%fused_computation.7 | convolution fusion | flops 1812529152 | bytes 6291464 | tf_op jit(solution)/shard_map/dot_general | solution.py:124
  104.6 0.6 copy.20
  105.2 3.6 %fusion.50 = (f32[4,512]{1,0:T(4,128)S(1)}, f32[4,512,512]{1,2,0:T(8,128)}) fusion(pred[512,512]{0,1:T(8,128)(4,1)S(1)} %broadcast_compare_fusion, bf16[512,3,4,96]{0,3,2,1:T(8,128)(2,1)S(1)} %bitcast.67), kind=kOutput, calls=%fused_computation.173 | convolution fusion | flops 205521408 | bytes 5251072 | tf_op jit(solution)/shard_map/while/body/eval_jaxpr/sub | solution.py:82
  108.9 2.7 %fusion.14 = bf16[4,96,512]{2,1,0:T(8,128)(2,1)S(1)} fusion(f32[4,512,512]{1,2,0:T(8,128)} %get-tuple-element.103, f32[4,512]{1,0:T(4,128)S(1)} %get-tuple-element.102, bf16[512,3,4,96]{0,3,2,1:T(8,128)(2,1)S(1)} %bitcast.68), kind=kOutput, calls=%fused_computation.17 | convolution fusion | flops 203620352 | bytes 4988928 | tf_op jit(solution)/shard_map/while/body/eval_jaxpr/hqk,khe->qhe/dot_general | solution.py:84
  111.6 2.3 %convolution_convert_fusion.1 = bf16[512,1536]{1,0:T(8,128)(2,1)S(1)} fusion(bf16[512,384]{0,1:T(8,128)(2,1)S(1)} %bitcast.71, bf16[384,1536]{0,1:T(8,128)(2,1)} %all-gather.4.cloned.1.call-done), kind=kOutput, calls=%fused_computation.9 | convolution fusion | flops 604766208 | bytes 3145728 | tf_op jit(solution)/shard_map/dot_general | solution.py:130
  114.1 3.0 %collective-permute-start.10 = (bf16[128,1536]{1,0:T(8,128)(2,1)S(1)}, bf16[128,1536]{1,0:T(8,128)(2,1)S(1)}, u32[]{:S(2)}, u32[]{:S(2)}) collective-permute-start(bf16[128,1536]{1,0:T(8,128)(2,1)S(1)} %get-tuple-element.68), channel_id=1, source_target_pairs={{0,1},{1,2},{2,3},{3,0},{4,5},{5,6},{6,7},{7,4},{8,9},{9,10},{10,1... | collective-permute-start | bytes 1179656 | tf_op jit(solution)/shard_map/ppermute | solution.py:57
  117.6 0.7 convert_reduce_fusion.2
  118.4 0.7 slice_compare_fusion.30
  119.1 6.3 %collective-permute-done.10 = bf16[128,1536]{1,0:T(8,128)(2,1)S(1)} collective-permute-done((bf16[128,1536]{1,0:T(8,128)(2,1)S(1)}, bf16[128,1536]{1,0:T(8,128)(2,1)S(1)}, u32[]{:S(2)}, u32[]{:S(2)}) %collective-permute-start.10) | collective-permute-done | bytes 393248 | tf_op jit(solution)/shard_map/ppermute | solution.py:57
  125.4 9.0 %collective-permute-done.11 = bf16[128,1536]{1,0:T(8,128)(2,1)} collective-permute-done((bf16[128,1536]{1,0:T(8,128)(2,1)S(1)}, bf16[128,1536]{1,0:T(8,128)(2,1)}, u32[]{:S(2)}, u32[]{:S(2)}) %collective-permute-start.11) | collective-permute-done | bytes 393248 | tf_op jit(solution)/shard_map/ppermute | solution.py:57
  134.4 0.6 collective-permute-done.12
  135.0 1.5 convert_reduce_fusion
  136.8 0.9 constant_dynamic-update-slice_fusion.31
  137.7 0.7 slice_compare_fusion.29
  138.4 1.5 collective-permute-start.14
  139.9 0.7 convert_reduce_fusion.33
  140.6 0.7 convert_reduce_fusion.34
  141.3 2.0 collective-permute-start.15
  143.3 5.6 %collective-permute-done.13 = bf16[128,1536]{1,0:T(8,128)(2,1)S(1)} collective-permute-done((bf16[128,1536]{1,0:T(8,128)(2,1)S(1)}, bf16[128,1536]{1,0:T(8,128)(2,1)S(1)}, u32[]{:S(2)}, u32[]{:S(2)}) %collective-permute-start.13) | collective-permute-done | bytes 393248 | tf_op jit(solution)/shard_map/ppermute | solution.py:44
  149.0 0.8 constant_dynamic-update-slice_fusion.30
  149.7 0.8 constant_dynamic-update-slice_fusion.29
  150.5 6.6 %collective-permute-done.15 = bf16[128,1536]{1,0:T(8,128)(2,1)S(1)} collective-permute-done((bf16[128,1536]{1,0:T(8,128)(2,1)S(1)}, bf16[128,1536]{1,0:T(8,128)(2,1)S(1)}, u32[]{:S(2)}, u32[]{:S(2)}) %collective-permute-start.15) | collective-permute-done | bytes 393248 | tf_op jit(solution)/shard_map/ppermute | solution.py:44
  157.2 0.8 constant_dynamic-update-slice_fusion.28
  158.0 0.8 constant_dynamic-update-slice_fusion.27
  158.7 0.8 constant_dynamic-update-slice_fusion.26
  159.5 0.8 constant_dynamic-update-slice_fusion.25
  160.3 0.8 constant_dynamic-update-slice_fusion.24
  161.1 3.5 %fusion.11 = f32[512,768]{1,0:T(8,128)S(1)} fusion(bf16[1536,768]{1,0:T(8,128)(2,1)} %all-gather.6.cloned.1.call-done, bf16[1024,1536]{1,0:T(8,128)(2,1)} %constant_dynamic-update-slice_fusion.24, s32[]{:T(128)S(6)} %select_n.159), kind=kOutput, calls=%fused_computation.14 | convolution fusion | flops 1207959552 | bytes 5505028 | tf_op jit(solution)/shard_map/dot_general | solution.py:135
  164.6 0.9 reshape.147
  165.9 1.2 fusion.49
  167.3 8.4 %all-gather.8.cloned.1.call-done = bf16[384,1536]{0,1:T(8,128)(2,1)} async-done(((bf16[384,192]{0,1:T(8,128)(2,1)}), bf16[384,1536]{0,1:T(8,128)(2,1)}) %all-gather.8.cloned.1.call-update) | async-done | bytes 1179664 | tf_op jit(solution)/shard_map/all_gather | solution.py:118
  176.1 8.1 %convolution_convert_fusion = bf16[512,1536]{1,0:T(8,128)(2,1)S(1)} fusion(bf16[384,1536]{0,1:T(8,128)(2,1)} %all-gather.8.cloned.1.call-done, bf16[512,384]{1,0:T(8,128)(2,1)S(1)} %fusion.37, f32[384]{0:T(512)S(1)} %copy-done.31, f32[384]{0:T(512)S(1)} %copy-done.32, f32[384]{0:T(512)S(1)} %get-tuple-element.18, f32[384]{0:T(512)S(1)} %get-tuple-element.19, ...), kind=kOutput, calls=%fused_computation.8 | convolution fusion | flops 629932032 | bytes 3209216 | tf_op jit(solution)/shard_map/dot_general | solution.py:145
  184.3 3.0 %collective-permute-start.16 = (bf16[128,1536]{1,0:T(8,128)(2,1)S(1)}, bf16[128,1536]{1,0:T(8,128)(2,1)S(1)}, u32[]{:S(2)}, u32[]{:S(2)}) collective-permute-start(bf16[128,1536]{1,0:T(8,128)(2,1)S(1)} %get-tuple-element.63), channel_id=1, source_target_pairs={{0,1},{1,2},{2,3},{3,0},{4,5},{5,6},{6,7},{7,4},{8,9},{9,10},{10,1... | collective-permute-start | bytes 1179656 | tf_op jit(solution)/shard_map/ppermute | solution.py:57
  187.8 7.9 %collective-permute-done.16 = bf16[128,1536]{1,0:T(8,128)(2,1)S(1)} collective-permute-done((bf16[128,1536]{1,0:T(8,128)(2,1)S(1)}, bf16[128,1536]{1,0:T(8,128)(2,1)S(1)}, u32[]{:S(2)}, u32[]{:S(2)}) %collective-permute-start.16) | collective-permute-done | bytes 393248 | tf_op jit(solution)/shard_map/ppermute | solution.py:57
  195.7 9.1 %collective-permute-done.17 = bf16[128,1536]{1,0:T(8,128)(2,1)S(1)} collective-permute-done((bf16[128,1536]{1,0:T(8,128)(2,1)S(1)}, bf16[128,1536]{1,0:T(8,128)(2,1)S(1)}, u32[]{:S(2)}, u32[]{:S(2)}) %collective-permute-start.17) | collective-permute-done | bytes 393248 | tf_op jit(solution)/shard_map/ppermute | solution.py:57
  204.8 0.6 collective-permute-done.18
  205.4 1.0 fusion.36
  (141 shorter events, 3.6 us)
Async XLA Ops:
  6.5 15.9 %copy-start.46 = (s32[1,4]{1,0:T(1,128)S(1)}, s32[1,4]{1,0:T(1,128)}, u32[]{:S(2)}) copy-start(s32[1,4]{1,0:T(1,128)} %param.10) | copy-start | bytes 52
  6.5 105.0 %all-gather.4.cloned.1.call-start = ((), (), s32[]{:S(2)}) async-start(), calls=%async_computation | async-start | bytes 1327104 | tf_op jit(solution)/shard_map/all_gather | solution.py:114
  7.3 153.8 %all-gather.6.cloned.1.call-start = ((), (), s32[]{:S(2)}) async-start(), calls=%async_computation.1 | async-start | bytes 2654208 | tf_op jit(solution)/shard_map/all_gather | solution.py:115
  9.0 166.7 %all-gather.8.cloned.1.call-start = ((), (), s32[]{:S(2)}) async-start(), calls=%async_computation.2 | async-start | bytes 1327104 | tf_op jit(solution)/shard_map/all_gather | solution.py:118
  13.4 10.0 %collective-permute-start = (bf16[128,1536]{1,0:T(8,128)(2,1)S(1)}, bf16[128,1536]{1,0:T(8,128)(2,1)S(1)}, u32[]{:S(2)}, u32[]{:S(2)}) collective-permute-start(bf16[128,1536]{1,0:T(8,128)(2,1)S(1)} %get-tuple-element.62), channel_id=1, source_target_pairs={{0,3},{1,0},{2,1},{3,2},{4,7},{5,4},{6,5},{7,6},{8,11},{9,8},{10,9... | collective-permute-start | bytes 1179656 | tf_op jit(solution)/shard_map/ppermute | solution.py:44
  13.6 22.3 %collective-permute-start.3 = (bf16[192,1152]{1,0:T(8,128)(2,1)S(1)}, bf16[192,1152]{1,0:T(8,128)(2,1)S(1)}, u32[]{:S(2)}, u32[]{:S(2)}) collective-permute-start(bf16[192,1152]{1,0:T(8,128)(2,1)S(1)} %bitcast.63), channel_id=1, source_target_pairs={{0,4},{4,8},{8,12},{12,16},{16,20},{20,24},{24,28},{28,0},{1,5},{5... | collective-permute-start | bytes 1327112 | tf_op jit(solution)/shard_map/ppermute | solution.py:16
  16.3 35.2 %collective-permute-start.7 = (bf16[192,1152]{1,0:T(8,128)(2,1)S(1)}, bf16[192,1152]{1,0:T(8,128)(2,1)S(1)}, u32[]{:S(2)}, u32[]{:S(2)}) collective-permute-start(bf16[192,1152]{1,0:T(8,128)(2,1)S(1)} %bitcast.64), channel_id=1, source_target_pairs={{0,28},{4,0},{8,4},{12,8},{16,12},{20,16},{24,20},{28,24},{1,29},{... | collective-permute-start | bytes 1327112 | tf_op jit(solution)/shard_map/ppermute | solution.py:19
  19.4 18.7 %collective-permute-start.1 = (bf16[128,1536]{1,0:T(8,128)(2,1)S(1)}, bf16[128,1536]{1,0:T(8,128)(2,1)S(1)}, u32[]{:S(2)}, u32[]{:S(2)}) collective-permute-start(bf16[128,1536]{1,0:T(8,128)(2,1)S(1)} %get-tuple-element.62), channel_id=1, source_target_pairs={{0,2},{1,3},{2,0},{3,1},{4,6},{5,7},{6,4},{7,5},{8,10},{9,11},{10,... | collective-permute-start | bytes 1179656 | tf_op jit(solution)/shard_map/ppermute | solution.py:44
  20.6 18.2 %collective-permute-start.2 = (bf16[128,1536]{1,0:T(8,128)(2,1)S(1)}, bf16[128,1536]{1,0:T(8,128)(2,1)S(1)}, u32[]{:S(2)}, u32[]{:S(2)}) collective-permute-start(bf16[128,1536]{1,0:T(8,128)(2,1)S(1)} %get-tuple-element.62), channel_id=1, source_target_pairs={{0,1},{1,2},{2,3},{3,0},{4,5},{5,6},{6,7},{7,4},{8,9},{9,10},{10,1... | collective-permute-start | bytes 1179656 | tf_op jit(solution)/shard_map/ppermute | solution.py:44
  35.9 14.0 %collective-permute-start.4 = (bf16[192,1152]{1,0:T(8,128)(2,1)S(1)}, bf16[192,1152]{1,0:T(8,128)(2,1)S(1)}, u32[]{:S(2)}, u32[]{:S(2)}) collective-permute-start(bf16[192,1152]{1,0:T(8,128)(2,1)S(1)} %collective-permute-done.3), channel_id=1, source_target_pairs={{0,4},{4,8},{8,12},{12,16},{16,20},{20,24},{24,28},{28,0},{1,5},{5... | collective-permute-start | bytes 1327112 | tf_op jit(solution)/shard_map/ppermute | solution.py:16
  49.9 22.6 %collective-permute-start.5 = (bf16[192,1152]{1,0:T(8,128)(2,1)S(1)}, bf16[192,1152]{1,0:T(8,128)(2,1)S(1)}, u32[]{:S(2)}, u32[]{:S(2)}) collective-permute-start(bf16[192,1152]{1,0:T(8,128)(2,1)S(1)} %collective-permute-done.4), channel_id=1, source_target_pairs={{0,4},{4,8},{8,12},{12,16},{16,20},{20,24},{24,28},{28,0},{1,5},{5... | collective-permute-start | bytes 1327112 | tf_op jit(solution)/shard_map/ppermute | solution.py:16
  51.5 25.2 %collective-permute-start.8 = (bf16[192,1152]{1,0:T(8,128)(2,1)S(1)}, bf16[192,1152]{1,0:T(8,128)(2,1)S(1)}, u32[]{:S(2)}, u32[]{:S(2)}) collective-permute-start(bf16[192,1152]{1,0:T(8,128)(2,1)S(1)} %collective-permute-done.7), channel_id=1, source_target_pairs={{0,28},{4,0},{8,4},{12,8},{16,12},{20,16},{24,20},{28,24},{1,29},{... | collective-permute-start | bytes 1327112 | tf_op jit(solution)/shard_map/ppermute | solution.py:19
  72.5 23.3 %collective-permute-start.6 = (bf16[192,1152]{1,0:T(8,128)(2,1)S(1)}, bf16[192,1152]{1,0:T(8,128)(2,1)S(1)}, u32[]{:S(2)}, u32[]{:S(2)}) collective-permute-start(bf16[192,1152]{1,0:T(8,128)(2,1)S(1)} %collective-permute-done.5), channel_id=1, source_target_pairs={{0,4},{4,8},{8,12},{12,16},{16,20},{20,24},{24,28},{28,0},{1,5},{5... | collective-permute-start | bytes 1327112 | tf_op jit(solution)/shard_map/ppermute | solution.py:16
  76.6 23.7 %collective-permute-start.9 = (bf16[192,1152]{1,0:T(8,128)(2,1)S(1)}, bf16[192,1152]{1,0:T(8,128)(2,1)S(1)}, u32[]{:S(2)}, u32[]{:S(2)}) collective-permute-start(bf16[192,1152]{1,0:T(8,128)(2,1)S(1)} %collective-permute-done.8), channel_id=1, source_target_pairs={{0,28},{4,0},{8,4},{12,8},{16,12},{20,16},{24,20},{28,24},{1,29},{... | collective-permute-start | bytes 1327112 | tf_op jit(solution)/shard_map/ppermute | solution.py:19
  111.5 23.5 %copy-start = (bf16[1,128,1536]{2,1,0:T(8,128)(2,1)S(1)}, bf16[1,128,1536]{2,1,0:T(8,128)(2,1)}, u32[]{:S(2)}) copy-start(bf16[1,128,1536]{2,1,0:T(8,128)(2,1)} %param.9) | copy-start | bytes 1179652
  113.9 22.9 %copy-start.4 = (f32[1536]{0:T(1024)S(1)}, f32[1536]{0:T(1024)}, u32[]{:S(2)}) copy-start(f32[1536]{0:T(1024)} %param.12) | copy-start | bytes 18436
  114.1 11.3 %collective-permute-start.10 = (bf16[128,1536]{1,0:T(8,128)(2,1)S(1)}, bf16[128,1536]{1,0:T(8,128)(2,1)S(1)}, u32[]{:S(2)}, u32[]{:S(2)}) collective-permute-start(bf16[128,1536]{1,0:T(8,128)(2,1)S(1)} %get-tuple-element.68), channel_id=1, source_target_pairs={{0,1},{1,2},{2,3},{3,0},{4,5},{5,6},{6,7},{7,4},{8,9},{9,10},{10,1... | collective-permute-start | bytes 1179656 | tf_op jit(solution)/shard_map/ppermute | solution.py:57
  117.1 17.3 %collective-permute-start.11 = (bf16[128,1536]{1,0:T(8,128)(2,1)S(1)}, bf16[128,1536]{1,0:T(8,128)(2,1)}, u32[]{:S(2)}, u32[]{:S(2)}) collective-permute-start(bf16[128,1536]{1,0:T(8,128)(2,1)S(1)} %get-tuple-element.70), channel_id=1, source_target_pairs={{0,2},{1,3},{2,0},{3,1},{4,6},{5,7},{6,4},{7,5},{8,10},{9,11},{10,... | collective-permute-start | bytes 1179656 | tf_op jit(solution)/shard_map/ppermute | solution.py:57
  117.1 17.9 %collective-permute-start.12 = (bf16[128,1536]{1,0:T(8,128)(2,1)S(1)}, bf16[128,1536]{1,0:T(8,128)(2,1)}, u32[]{:S(2)}, u32[]{:S(2)}) collective-permute-start(bf16[128,1536]{1,0:T(8,128)(2,1)S(1)} %get-tuple-element.69), channel_id=1, source_target_pairs={{0,3},{1,0},{2,1},{3,2},{4,7},{5,4},{6,5},{7,6},{8,11},{9,8},{10,9... | collective-permute-start | bytes 1179656 | tf_op jit(solution)/shard_map/ppermute | solution.py:57
  117.6 22.3 %copy-start.2 = (bf16[31,384]{1,0:T(8,128)(2,1)S(1)}, bf16[31,384]{1,0:T(8,128)(2,1)}, u32[]{:S(2)}) copy-start(bf16[31,384]{1,0:T(8,128)(2,1)} %param.16) | copy-start | bytes 71428
  137.7 11.2 %collective-permute-start.13 = (bf16[128,1536]{1,0:T(8,128)(2,1)S(1)}, bf16[128,1536]{1,0:T(8,128)(2,1)S(1)}, u32[]{:S(2)}, u32[]{:S(2)}) collective-permute-start(bf16[128,1536]{1,0:T(8,128)(2,1)S(1)} %get-tuple-element.58), channel_id=1, source_target_pairs={{0,3},{1,0},{2,1},{3,2},{4,7},{5,4},{6,5},{7,6},{8,11},{9,8},{10,9... | collective-permute-start | bytes 1179656 | tf_op jit(solution)/shard_map/ppermute | solution.py:44
  138.4 11.3 %collective-permute-start.14 = (bf16[128,1536]{1,0:T(8,128)(2,1)S(1)}, bf16[128,1536]{1,0:T(8,128)(2,1)S(1)}, u32[]{:S(2)}, u32[]{:S(2)}) collective-permute-start(bf16[128,1536]{1,0:T(8,128)(2,1)S(1)} %get-tuple-element.58), channel_id=1, source_target_pairs={{0,2},{1,3},{2,0},{3,1},{4,6},{5,7},{6,4},{7,5},{8,10},{9,11},{10,... | collective-permute-start | bytes 1179656 | tf_op jit(solution)/shard_map/ppermute | solution.py:44
  141.3 15.9 %collective-permute-start.15 = (bf16[128,1536]{1,0:T(8,128)(2,1)S(1)}, bf16[128,1536]{1,0:T(8,128)(2,1)S(1)}, u32[]{:S(2)}, u32[]{:S(2)}) collective-permute-start(bf16[128,1536]{1,0:T(8,128)(2,1)S(1)} %get-tuple-element.58), channel_id=1, source_target_pairs={{0,1},{1,2},{2,3},{3,0},{4,5},{5,6},{6,7},{7,4},{8,9},{9,10},{10,1... | collective-permute-start | bytes 1179656 | tf_op jit(solution)/shard_map/ppermute | solution.py:44
  165.5 10.3 %copy-start.5 = (f32[384]{0:T(512)S(1)}, f32[384]{0:T(512)}, u32[]{:S(2)}) copy-start(f32[384]{0:T(512)} %get-tuple-element.28) | copy-start | bytes 4612
  165.5 10.3 %copy-start.6 = (f32[384]{0:T(512)S(1)}, f32[384]{0:T(512)}, u32[]{:S(2)}) copy-start(f32[384]{0:T(512)} %get-tuple-element.30) | copy-start | bytes 4612
  165.5 10.2 %copy-start.7 = (f32[384]{0:T(512)S(1)}, f32[384]{0:T(512)}, u32[]{:S(2)}) copy-start(f32[384]{0:T(512)} %get-tuple-element.32) | copy-start | bytes 4612
  165.5 10.2 %copy-start.8 = (f32[384]{0:T(512)S(1)}, f32[384]{0:T(512)}, u32[]{:S(2)}) copy-start(f32[384]{0:T(512)} %get-tuple-element.33) | copy-start | bytes 4612
  165.5 10.2 %copy-start.9 = (f32[384]{0:T(512)S(1)}, f32[384]{0:T(512)}, u32[]{:S(2)}) copy-start(f32[384]{0:T(512)} %get-tuple-element.34) | copy-start | bytes 4612
  165.5 10.2 %copy-start.10 = (f32[384]{0:T(512)S(1)}, f32[384]{0:T(512)}, u32[]{:S(2)}) copy-start(f32[384]{0:T(512)} %get-tuple-element.35) | copy-start | bytes 4612
  165.5 10.2 %copy-start.11 = (f32[384]{0:T(512)S(1)}, f32[384]{0:T(512)}, u32[]{:S(2)}) copy-start(f32[384]{0:T(512)} %get-tuple-element.36) | copy-start | bytes 4612
  165.5 10.2 %copy-start.12 = (f32[384]{0:T(512)S(1)}, f32[384]{0:T(512)}, u32[]{:S(2)}) copy-start(f32[384]{0:T(512)} %get-tuple-element.37) | copy-start | bytes 4612
  165.6 10.2 %copy-start.13 = (f32[384]{0:T(512)S(1)}, f32[384]{0:T(512)}, u32[]{:S(2)}) copy-start(f32[384]{0:T(512)} %get-tuple-element.38) | copy-start | bytes 4612
  165.6 10.2 %copy-start.14 = (f32[384]{0:T(512)S(1)}, f32[384]{0:T(512)}, u32[]{:S(2)}) copy-start(f32[384]{0:T(512)} %get-tuple-element.39) | copy-start | bytes 4612
  165.6 10.2 %copy-start.15 = (f32[384]{0:T(512)S(1)}, f32[384]{0:T(512)}, u32[]{:S(2)}) copy-start(f32[384]{0:T(512)} %get-tuple-element.40) | copy-start | bytes 4612
  165.6 10.2 %copy-start.16 = (f32[384]{0:T(512)S(1)}, f32[384]{0:T(512)}, u32[]{:S(2)}) copy-start(f32[384]{0:T(512)} %get-tuple-element.41) | copy-start | bytes 4612
  165.6 10.2 %copy-start.17 = (f32[384]{0:T(512)S(1)}, f32[384]{0:T(512)}, u32[]{:S(2)}) copy-start(f32[384]{0:T(512)} %get-tuple-element.42) | copy-start | bytes 4612
  165.6 10.2 %copy-start.18 = (f32[384]{0:T(512)S(1)}, f32[384]{0:T(512)}, u32[]{:S(2)}) copy-start(f32[384]{0:T(512)} %get-tuple-element.43) | copy-start | bytes 4612
  165.6 10.2 %copy-start.19 = (f32[384]{0:T(512)S(1)}, f32[384]{0:T(512)}, u32[]{:S(2)}) copy-start(f32[384]{0:T(512)} %get-tuple-element.44) | copy-start | bytes 4612
  165.6 10.2 %copy-start.21 = (f32[384]{0:T(512)S(1)}, f32[384]{0:T(512)}, u32[]{:S(2)}) copy-start(f32[384]{0:T(512)} %get-tuple-element.45) | copy-start | bytes 4612
  165.6 10.2 %copy-start.22 = (f32[384]{0:T(512)S(1)}, f32[384]{0:T(512)}, u32[]{:S(2)}) copy-start(f32[384]{0:T(512)} %get-tuple-element.46) | copy-start | bytes 4612
  165.6 10.2 %copy-start.23 = (f32[384]{0:T(512)S(1)}, f32[384]{0:T(512)}, u32[]{:S(2)}) copy-start(f32[384]{0:T(512)} %get-tuple-element.47) | copy-start | bytes 4612
  165.7 10.2 %copy-start.24 = (f32[384]{0:T(512)S(1)}, f32[384]{0:T(512)}, u32[]{:S(2)}) copy-start(f32[384]{0:T(512)} %get-tuple-element.48) | copy-start | bytes 4612
  165.7 10.2 %copy-start.25 = (f32[384]{0:T(512)S(1)}, f32[384]{0:T(512)}, u32[]{:S(2)}) copy-start(f32[384]{0:T(512)} %get-tuple-element.49) | copy-start | bytes 4612
  165.7 10.2 %copy-start.26 = (f32[384]{0:T(512)S(1)}, f32[384]{0:T(512)}, u32[]{:S(2)}) copy-start(f32[384]{0:T(512)} %get-tuple-element.50) | copy-start | bytes 4612
  165.7 10.2 %copy-start.27 = (f32[384]{0:T(512)S(1)}, f32[384]{0:T(512)}, u32[]{:S(2)}) copy-start(f32[384]{0:T(512)} %get-tuple-element.51) | copy-start | bytes 4612
  165.7 10.2 %copy-start.28 = (f32[384]{0:T(512)S(1)}, f32[384]{0:T(512)}, u32[]{:S(2)}) copy-start(f32[384]{0:T(512)} %get-tuple-element.52) | copy-start | bytes 4612
  165.7 10.2 %copy-start.29 = (f32[384]{0:T(512)S(1)}, f32[384]{0:T(512)}, u32[]{:S(2)}) copy-start(f32[384]{0:T(512)} %get-tuple-element.53) | copy-start | bytes 4612
  165.7 10.2 %copy-start.30 = (f32[384]{0:T(512)S(1)}, f32[384]{0:T(512)}, u32[]{:S(2)}) copy-start(f32[384]{0:T(512)} %get-tuple-element.54) | copy-start | bytes 4612
  165.7 10.2 %copy-start.31 = (f32[384]{0:T(512)S(1)}, f32[384]{0:T(512)}, u32[]{:S(2)}) copy-start(f32[384]{0:T(512)} %get-tuple-element.55) | copy-start | bytes 4612
  165.7 10.2 %copy-start.32 = (f32[384]{0:T(512)S(1)}, f32[384]{0:T(512)}, u32[]{:S(2)}) copy-start(f32[384]{0:T(512)} %get-tuple-element.56) | copy-start | bytes 4612
  165.7 10.2 %copy-start.33 = (pred[512]{0:T(512)(128)(4,1)S(1)}, pred[512]{0:T(512)(128)(4,1)}, u32[]{:S(2)}) copy-start(pred[512]{0:T(512)(128)(4,1)} %get-tuple-element.71) | copy-start | bytes 1540
  165.8 10.2 %copy-start.34 = (pred[512]{0:T(512)(128)(4,1)S(1)}, pred[512]{0:T(512)(128)(4,1)}, u32[]{:S(2)}) copy-start(pred[512]{0:T(512)(128)(4,1)} %get-tuple-element.72) | copy-start | bytes 1540
  165.8 10.2 %copy-start.35 = (pred[512]{0:T(512)(128)(4,1)S(1)}, pred[512]{0:T(512)(128)(4,1)}, u32[]{:S(2)}) copy-start(pred[512]{0:T(512)(128)(4,1)} %get-tuple-element.73) | copy-start | bytes 1540
  165.8 10.2 %copy-start.36 = (pred[512]{0:T(512)(128)(4,1)S(1)}, pred[512]{0:T(512)(128)(4,1)}, u32[]{:S(2)}) copy-start(pred[512]{0:T(512)(128)(4,1)} %get-tuple-element.74) | copy-start | bytes 1540
  165.8 10.2 %copy-start.37 = (pred[512]{0:T(512)(128)(4,1)S(1)}, pred[512]{0:T(512)(128)(4,1)}, u32[]{:S(2)}) copy-start(pred[512]{0:T(512)(128)(4,1)} %get-tuple-element.75) | copy-start | bytes 1540
  165.8 10.2 %copy-start.38 = (pred[512]{0:T(512)(128)(4,1)S(1)}, pred[512]{0:T(512)(128)(4,1)}, u32[]{:S(2)}) copy-start(pred[512]{0:T(512)(128)(4,1)} %get-tuple-element.76) | copy-start | bytes 1540
  165.8 10.2 %copy-start.39 = (pred[512]{0:T(512)(128)(4,1)S(1)}, pred[512]{0:T(512)(128)(4,1)}, u32[]{:S(2)}) copy-start(pred[512]{0:T(512)(128)(4,1)} %get-tuple-element.77) | copy-start | bytes 1540
  165.8 10.2 %copy-start.40 = (pred[512]{0:T(512)(128)(4,1)S(1)}, pred[512]{0:T(512)(128)(4,1)}, u32[]{:S(2)}) copy-start(pred[512]{0:T(512)(128)(4,1)} %get-tuple-element.78) | copy-start | bytes 1540
  165.8 10.2 %copy-start.41 = (pred[512]{0:T(512)(128)(4,1)S(1)}, pred[512]{0:T(512)(128)(4,1)}, u32[]{:S(2)}) copy-start(pred[512]{0:T(512)(128)(4,1)} %get-tuple-element.79) | copy-start | bytes 1540
  165.8 10.2 %copy-start.42 = (pred[512]{0:T(512)(128)(4,1)S(1)}, pred[512]{0:T(512)(128)(4,1)}, u32[]{:S(2)}) copy-start(pred[512]{0:T(512)(128)(4,1)} %get-tuple-element.80) | copy-start | bytes 1540
  165.8 10.2 %copy-start.43 = (pred[512]{0:T(512)(128)(4,1)S(1)}, pred[512]{0:T(512)(128)(4,1)}, u32[]{:S(2)}) copy-start(pred[512]{0:T(512)(128)(4,1)} %get-tuple-element.81) | copy-start | bytes 1540
  184.3 11.4 %collective-permute-start.16 = (bf16[128,1536]{1,0:T(8,128)(2,1)S(1)}, bf16[128,1536]{1,0:T(8,128)(2,1)S(1)}, u32[]{:S(2)}, u32[]{:S(2)}) collective-permute-start(bf16[128,1536]{1,0:T(8,128)(2,1)S(1)} %get-tuple-element.63), channel_id=1, source_target_pairs={{0,1},{1,2},{2,3},{3,0},{4,5},{5,6},{6,7},{7,4},{8,9},{9,10},{10,1... | collective-permute-start | bytes 1179656 | tf_op jit(solution)/shard_map/ppermute | solution.py:57
  187.4 17.5 %collective-permute-start.17 = (bf16[128,1536]{1,0:T(8,128)(2,1)S(1)}, bf16[128,1536]{1,0:T(8,128)(2,1)S(1)}, u32[]{:S(2)}, u32[]{:S(2)}) collective-permute-start(bf16[128,1536]{1,0:T(8,128)(2,1)S(1)} %get-tuple-element.65), channel_id=1, source_target_pairs={{0,2},{1,3},{2,0},{3,1},{4,6},{5,7},{6,4},{7,5},{8,10},{9,11},{10,... | collective-permute-start | bytes 1179656 | tf_op jit(solution)/shard_map/ppermute | solution.py:57
  187.6 17.8 %collective-permute-start.18 = (bf16[128,1536]{1,0:T(8,128)(2,1)S(1)}, bf16[128,1536]{1,0:T(8,128)(2,1)S(1)}, u32[]{:S(2)}, u32[]{:S(2)}) collective-permute-start(bf16[128,1536]{1,0:T(8,128)(2,1)S(1)} %get-tuple-element.64), channel_id=1, source_target_pairs={{0,3},{1,0},{2,1},{3,2},{4,7},{5,4},{6,5},{7,6},{8,11},{9,8},{10,9... | collective-permute-start | bytes 1179656 | tf_op jit(solution)/shard_map/ppermute | solution.py:57
  (5 other events, 29.9 us)
Sparse Core Ops, SparseCore 0:
  9.5 65.5 all-gather.3
  77.3 56.6 all-gather.5
  136.2 39.4 all-gather.7
